TPU v7x, 32 devices: a whole 2x2x4 slice. The times are simulated.
32 devices in a mesh: band: 16 (over z, x, core), chan: 2 (over y).
Axes of the slice: x: 2, y: 2, z: 4, core: 2. Of those that a mesh axis runs over, the one named last changes fastest.
Arguments:
- features: bfloat16 [256, 64, 1024], P('chan', 'band'), may hold values from -6 to 6
- depth_kernel: bfloat16 [3, 9, 256], P(None, None, 'chan'), may hold values from -2 to 2
- pointwise: bfloat16 [4, 256, 256], P(None, 'chan'), may hold values from -0.25 to 0.25
- cotangent: bfloat16 [256, 64, 1024], P('chan', 'band'), may hold values from -6 to 6
Outputs:
- output: bfloat16 [256, 64, 1024], P('chan', 'band')
- grad_input: float32 [256, 64, 1024], P('chan', 'band')
- grad_depth: float32 [3, 9, 256], P(None, None, 'chan')
- grad_point: float32 [4, 256, 256], P(None, 'chan')
All inputs are finite; a program needn't handle non-finite values.
Results may differ from a plain program's by a relative error of at most 0.0057.
Values may be sent and summed in bfloat16 or wider, within the bound.
No kernel may reach another device: no remote copies, remote signals or barrier semaphores. Data moves between devices by JAX's collectives and lax.ppermute only.
A program may use at most 128 MiB of HBM per device.

v0:
```python
import jax
import jax.numpy as jnp
from jax import lax
from jax.sharding import PartitionSpec as P

GSCALE = 1024
dilations = (6, 12, 18)


def shifted(block, axis, distance):
    devices = range(lax.axis_size(axis))
    route = [(i - distance, i) for i in devices if i - distance in devices]
    if not route:
        return jnp.zeros_like(block)
    return lax.ppermute(block, axis, route)


def from_device(block, ahead):
    return block if ahead == 0 else shifted(block, "band", -ahead)


def rows_at(field, offset):
    height = field.shape[1]
    ahead, start = divmod(offset, height)
    if start == 0:
        return from_device(field, ahead)
    return jnp.concatenate(
        [from_device(field[:, start:], ahead), from_device(field[:, :start], ahead + 1)], axis=1
    )


def local(features, depth_kernel, pointwise, cotangent):
    kernel = depth_kernel.astype(jnp.float32)
    feat_rows = {0: features}
    for spacing in dilations:
        for side in (-1, 1):
            feat_rows[side * spacing] = rows_at(features, side * spacing)
    feat_rows = {k: v.astype(jnp.float32) for k, v in feat_rows.items()}
    branches = [features]
    for which, spacing in enumerate(dilations):
        total = jnp.zeros(features.shape, jnp.float32)
        for tap_index in range(9):
            row_step = tap_index // 3 - 1
            col_step = tap_index % 3 - 1
            total = total + kernel[which, tap_index][:, None, None] * jnp.roll(
                feat_rows[row_step * spacing], -col_step * spacing, axis=-1
            )
        branches.append(total.astype(jnp.bfloat16))
    stacked = jnp.stack(branches)
    output = lax.psum_scatter(
        jnp.einsum("bchw,bco->ohw", stacked, pointwise, preferred_element_type=jnp.float32).astype(
            jnp.bfloat16
        ),
        "chan",
        scatter_dimension=0,
        tiled=True,
    )
    cot_full = lax.all_gather(cotangent, "chan", axis=0, tiled=True)
    grad_sum = jnp.einsum("bco,ohw->bchw", pointwise, cot_full, preferred_element_type=jnp.float32)
    point_local = jnp.einsum("bchw,ohw->bco", stacked, cot_full, preferred_element_type=jnp.float32)
    grad_branches = grad_sum.astype(jnp.bfloat16)
    grad_input = grad_branches[0].astype(jnp.float32)
    depth_rows = []
    for which, spacing in enumerate(dilations):
        grad_field = grad_branches[which + 1]
        grad_f = grad_field.astype(jnp.float32)
        grad_rows = {0: grad_f}
        for side in (-1, 1):
            grad_rows[side * spacing] = rows_at(grad_field, side * spacing).astype(jnp.float32)
        tap_rows = []
        for tap_index in range(9):
            row_step = tap_index // 3 - 1
            col_step = tap_index % 3 - 1
            grad_input = grad_input + kernel[which, tap_index][:, None, None] * jnp.roll(
                grad_rows[-row_step * spacing], col_step * spacing, axis=-1
            )
            tap_rows.append(
                jnp.sum(
                    grad_f * jnp.roll(feat_rows[row_step * spacing], -col_step * spacing, axis=-1),
                    axis=(1, 2),
                )
            )
        depth_rows.append(jnp.stack(tap_rows))
    depth_local = jnp.stack(depth_rows)
    flat = jnp.concatenate([depth_local.reshape(-1), point_local.reshape(-1)])
    flat = lax.psum(flat, "band")
    depth_total = flat[: depth_local.size].reshape(depth_local.shape)
    point_total = flat[depth_local.size :].reshape(point_local.shape)
    return (output, grad_input, depth_total / GSCALE, point_total / GSCALE)


def solution(mesh):
    return jax.shard_map(
        local,
        mesh=mesh,
        in_specs=(
            P("chan", "band", None),
            P(None, None, "chan"),
            P(None, "chan", None),
            P("chan", "band", None),
        ),
        out_specs=(
            P("chan", "band", None),
            P("chan", "band", None),
            P(None, None, "chan"),
            P(None, "chan", None),
        ),
        check_vma=False,
    )
```

profile of v0, /device:TPU:0, one launch (start us, length us, event | category | flops | bytes accessed | tf_op | source)
XLA Modules:
  0.0 347.8 jit_solution(9047192822826043685)
XLA Ops:
  7.2 2.0 copy.35
  10.2 1.3 collective-permute-start.8
  11.5 5.1 %collective-permute-start.6 = (bf16[128,2,1024]{0,2,1:T(8,128)(2,1)}, bf16[128,2,1024]{0,2,1:T(8,128)(2,1)S(1)}, u32[]{:S(2)}, u32[]{:S(2)}) collective-permute-start(bf16[128,2,1024]{0,2,1:T(8,128)(2,1)} %get-tuple-element.125), channel_id=1, source_target_pairs={{0,10},{2,12},{4,14},{6,16},{8,18},{10,20},{12,22},{14,24},{16,26}... | collective-permute-start | bytes 1572872 | tf_op jit(solution)/shard_map/ppermute | solution.py:15
  16.6 1.3 collective-permute-start.2
  17.9 7.0 %collective-permute-start = (bf16[128,2,1024]{0,2,1:T(8,128)(2,1)}, bf16[128,2,1024]{0,2,1:T(8,128)(2,1)}, u32[]{:S(2)}, u32[]{:S(2)}) collective-permute-start(bf16[128,2,1024]{0,2,1:T(8,128)(2,1)} %get-tuple-element.125), channel_id=1, source_target_pairs={{0,4},{2,6},{4,8},{6,10},{8,12},{10,14},{12,16},{14,18},{16,20},{1... | collective-permute-start | bytes 1572872 | tf_op jit(solution)/shard_map/ppermute | solution.py:15
  24.9 1.3 copy.43
  26.3 2.7 collective-permute-start.7
  30.2 1.2 slice_bitcast_fusion.30
  32.8 1.3 collective-permute-start.9
  34.1 7.1 %collective-permute-done.7 = bf16[128,2,1024]{0,2,1:T(8,128)(2,1)S(1)} collective-permute-done((bf16[128,2,1024]{0,2,1:T(8,128)(2,1)}, bf16[128,2,1024]{0,2,1:T(8,128)(2,1)S(1)}, u32[]{:S(2)}, u32[]{:S(2)}) %collective-permute-start.7) | collective-permute-done | bytes 524320 | tf_op jit(solution)/shard_map/ppermute | solution.py:15
  41.2 1.3 collective-permute-start.3
  42.7 2.3 fusion.104
  45.0 1.7 collective-permute-start.1
  46.7 1.3 collective-permute-start.5
  48.2 2.2 fusion.106
  50.4 19.0 %collective-permute-start.4 = (bf16[128,4,1024]{0,2,1:T(8,128)(2,1)S(1)}, bf16[128,4,1024]{0,2,1:T(8,128)(2,1)S(1)}, u32[]{:S(2)}, u32[]{:S(2)}) collective-permute-start(bf16[128,4,1024]{0,2,1:T(8,128)(2,1)S(1)} %copy.35), channel_id=1, source_target_pairs={{0,6},{2,8},{4,10},{6,12},{8,14},{10,16},{12,18},{14,20},{16,22},{... | collective-permute-start | bytes 3145736 | tf_op jit(solution)/shard_map/ppermute | solution.py:15
  69.4 1.4 maximum_convert_fusion.1
  72.0 1.6 maximum_convert_fusion
  74.7 7.1 %fusion.75 = bf16[1,128,4,1024]{1,3,0,2:T(8,128)(2,1)} fusion(f32[128,4,18]{0,2,1:T(8,128)S(1)} %get-tuple-element.90, f32[128,4,1006]{0,2,1:T(8,128)} %get-tuple-element.92, f32[128]{0:T(128)S(1)} %get-tuple-element.128, f32[128]{0:T(128)S(1)} %get-tuple-element.129, f32[128,4,1006]{0,2,1:T(8,128)} %get-tuple-element.91, ...), kind=kLoop, calls=%fused_computation.159 | loop fusion | flops 15204352 | bytes 16781824 | tf_op jit(solution)/shard_map/stack | solution.py:49
  82.0 5.8 %fusion.77 = bf16[1,128,4,1024]{1,3,0,2:T(8,128)(2,1)} fusion(f32[128,4,6]{0,2,1:T(8,128)S(1)} %get-tuple-element.82, f32[128,4,1018]{0,2,1:T(8,128)S(1)} %get-tuple-element.84, f32[128]{0:T(128)} %get-tuple-element.147, f32[128]{0:T(128)} %get-tuple-element.148, f32[128,4,1018]{0,2,1:T(8,128)S(1)} %get-tuple-element.83, ...), kind=kLoop, calls=%fused_computation.161 | loop fusion | flops 15204352 | bytes 16781824 | tf_op jit(solution)/shard_map/stack | solution.py:49
  87.9 9.6 %collective-permute-done.4 = bf16[128,4,1024]{0,2,1:T(8,128)(2,1)S(1)} collective-permute-done((bf16[128,4,1024]{0,2,1:T(8,128)(2,1)S(1)}, bf16[128,4,1024]{0,2,1:T(8,128)(2,1)S(1)}, u32[]{:S(2)}, u32[]{:S(2)}) %collective-permute-start.4) | collective-permute-done | bytes 1048608 | tf_op jit(solution)/shard_map/ppermute | solution.py:15
  97.9 2.1 fusion.120
  101.3 4.3 %fusion.76 = bf16[1,128,4,1024]{1,3,0,2:T(8,128)(2,1)} fusion(f32[128,4,12]{0,2,1:T(8,128)S(1)} %get-tuple-element.118, f32[128,4,1012]{0,2,1:T(8,128)S(1)} %get-tuple-element.120, f32[128]{0:T(128)S(1)} %copy-done.97, bf16[128,4,1024]{0,2,1:T(8,128)(2,1)S(1)} %collective-permute-done.5, f32[128]{0:T(128)S(1)} %copy-done.98, ...), kind=kLoop, calls=%fused_computation.160 | loop fusion | flops 14155776 | bytes 16781824 | tf_op jit(solution)/shard_map/stack | solution.py:49
  105.7 3.0 convolution_convert_fusion
  109.2 5.9 %fusion.47 = (f32[128]{0:T(128)}, f32[128]{0:T(128)}, f32[128]{0:T(128)}, f32[128]{0:T(128)}, f32[128]{0:T(128)}, /*index=5*/f32[128]{0:T(128)}) fusion(f32[128,4,1018]{0,2,1:T(8,128)S(1)} %copy-done.15, f32[128,4,6]{0,2,1:T(8,128)S(1)} %copy-done.84, bf16[4,128,4,1024]{1,3,2,0:T(8,128)(2,1)S(1)} %convolution_convert_fusion, ...), kind=kLoop, calls=%fused_computation.83 | loop fusion | flops 10484992 | bytes 14683136 | tf_op jit(solution)/shard_map/reduce_sum | solution.py:78
  115.1 1.3 fusion.72
  116.5 1.1 copy.58
  118.5 4.5 %fusion.48 = (f32[128]{0:T(128)}, f32[128]{0:T(128)}, f32[128]{0:T(128)}, f32[128]{0:T(128)}, f32[128]{0:T(128)}, /*index=5*/f32[128]{0:T(128)}, f32[128]{0:T(128)}) fusion(bf16[128,2,1024]{0,2,1:T(8,128)(2,1)S(1)} %copy-done.41, bf16[128,2,1024]{0,2,1:T(8,128)(2,1)} %collective-permute-done.2, bf16[4,128,4,1024]{1,3,2,0:T(8,128)(2,1)S(1)} %convolution_convert_fusion, ...), kind=kLoop, calls=%fused_computation.84 | loop fusion | flops 13630592 | bytes 13635072 | tf_op jit(solution)/shard_map/reduce_sum | solution.py:78
  123.1 4.9 %fusion.45 = (f32[128]{0:T(128)}, f32[128]{0:T(128)}, f32[128]{0:T(128)}, f32[128]{0:T(128)}, f32[128]{0:T(128)}, /*index=5*/f32[128]{0:T(128)}, f32[128]{0:T(128)}, f32[128]{0:T(128)}) fusion(bf16[128,4,1024]{0,2,1:T(8,128)(2,1)S(1)} %copy.35, bf16[4,128,4,1024]{1,3,2,0:T(8,128)(2,1)S(1)} %convolution_convert_fusion, f32[128,4,6]{0,2,1:T(8,128)S(1)} %copy-done.77, ...), kind=kLoop, calls=%fused_computation.81 | loop fusion | flops 13630464 | bytes 13635584 | tf_op jit(solution)/shard_map/reduce_sum | solution.py:78
  128.1 2.5 stack.142
  130.5 6.4 %fusion.49 = (f32[128]{0:T(128)}, f32[128]{0:T(128)}, f32[128]{0:T(128)}, f32[128]{0:T(128)}, f32[128]{0:T(128)}, /*index=5*/f32[128]{0:T(128)}) fusion(f32[128,4,6]{0,2,1:T(8,128)} %copy-done.78, f32[128,4,1018]{0,2,1:T(8,128)S(1)} %copy-done.13, bf16[4,128,4,1024]{1,3,2,0:T(8,128)(2,1)} %copy-done.2, f32[128,4,18]{0,2,1:T(8,128)} %copy-done.57, ...), kind=kLoop, calls=%fused_computation.85 | loop fusion | flops 11009280 | bytes 13634560 | tf_op jit(solution)/shard_map/reduce_sum | solution.py:78
  137.0 1.4 stack.131
  138.3 1.4 stack.153
  140.4 1.9 pad_maximum_fusion.21
  142.4 3.1 bitcast_convert_fusion
  145.5 3.0 copy.56
  148.5 3.9 %fusion.84 = (f32[128,4,1024]{0,2,1:T(8,128)S(1)}, f32[128,4,1024]{0,2,1:T(8,128)S(1)}, f32[128,4,1024]{0,2,1:T(8,128)S(1)}, bf16[128,4,1024]{0,2,1:T(8,128)(2,1...) fusion(bf16[4,128,4,1024]{1,3,2,0:T(8,128)(2,1)} %copy-done.2), kind=kLoop, calls=%fused_computation.199 | loop fusion | flops 1572864 | bytes 12582912 | tf_op jit(solution)/shard_map/convert_element_type | solution.py:66
  153.5 20.2 %collective-permute-start.18 = (bf16[128,2,1024]{0,2,1:T(8,128)(2,1)}, bf16[128,2,1024]{0,2,1:T(8,128)(2,1)S(1)}, u32[]{:S(2)}, u32[]{:S(2)}) collective-permute-start(bf16[128,2,1024]{0,2,1:T(8,128)(2,1)} %get-tuple-element.93), channel_id=1, source_target_pairs={{0,10},{2,12},{4,14},{6,16},{8,18},{10,20},{12,22},{14,24},{16,26}... | collective-permute-start | bytes 1572872 | tf_op jit(solution)/shard_map/ppermute | solution.py:15
  173.7 1.3 collective-permute-start.16
  175.0 5.6 %collective-permute-start.19 = (bf16[128,2,1024]{0,2,1:T(8,128)(2,1)}, bf16[128,2,1024]{0,2,1:T(8,128)(2,1)S(1)}, u32[]{:S(2)}, u32[]{:S(2)}) collective-permute-start(bf16[128,2,1024]{0,2,1:T(8,128)(2,1)} %get-tuple-element.94), channel_id=1, source_target_pairs={{0,8},{2,10},{4,12},{6,14},{8,16},{10,18},{12,20},{14,22},{16,24},... | collective-permute-start | bytes 1572872 | tf_op jit(solution)/shard_map/ppermute | solution.py:15
  180.6 1.3 collective-permute-start.17
  181.9 2.3 fusion.88
  184.2 2.4 fusion.92
  186.6 2.4 fusion.96
  190.0 2.9 collective-permute-start.12
  192.9 66.5 %all-reduce.2.cloned.1.call-done = f32[134528]{0:T(1024)} async-done(((f32[134528]{0:T(1024)}), f32[134528]{0:T(1024)}) %all-reduce.2.cloned.1.call-update) | async-done | bytes 538128 | tf_op jit(solution)/shard_map/psum | solution.py:86
  259.4 1.1 slice_multiply_fusion
  262.8 1.3 collective-permute-start.10
  264.1 3.1 collective-permute-start.13
  267.3 2.4 fusion.90
  269.7 1.3 collective-permute-start.11
  271.0 6.0 %collective-permute-start.15 = (bf16[128,4,1024]{0,2,1:T(8,128)(2,1)S(1)}, bf16[128,4,1024]{0,2,1:T(8,128)(2,1)S(1)}, u32[]{:S(2)}, u32[]{:S(2)}) collective-permute-start(bf16[128,4,1024]{0,2,1:T(8,128)(2,1)S(1)} %copy-done.54), channel_id=1, source_target_pairs={{0,6},{2,8},{4,10},{6,12},{8,14},{10,16},{12,18},{14,20},{16,22},{... | collective-permute-start | bytes 3145736 | tf_op jit(solution)/shard_map/ppermute | solution.py:15
  277.2 2.2 fusion.86
  279.4 1.3 collective-permute-start.14
  280.7 4.8 %collective-permute-done.11 = bf16[128,2,1024]{0,2,1:T(8,128)(2,1)S(1)} collective-permute-done((bf16[128,2,1024]{0,2,1:T(8,128)(2,1)}, bf16[128,2,1024]{0,2,1:T(8,128)(2,1)S(1)}, u32[]{:S(2)}, u32[]{:S(2)}) %collective-permute-start.11) | collective-permute-done | bytes 524320 | tf_op jit(solution)/shard_map/ppermute | solution.py:15
  285.7 1.4 maximum_convert_fusion.5
  288.3 24.8 %collective-permute-done.15 = bf16[128,4,1024]{0,2,1:T(8,128)(2,1)S(1)} collective-permute-done((bf16[128,4,1024]{0,2,1:T(8,128)(2,1)S(1)}, bf16[128,4,1024]{0,2,1:T(8,128)(2,1)S(1)}, u32[]{:S(2)}, u32[]{:S(2)}) %collective-permute-start.15) | collective-permute-done | bytes 1048608 | tf_op jit(solution)/shard_map/ppermute | solution.py:15
  313.2 2.2 fusion.111
  315.4 2.4 fusion.109
  317.8 1.3 copy-done.3
  320.4 15.6 %fusion.40 = f32[128,4,1024]{0,2,1:T(8,128)S(1)} fusion(f32[128,4,6]{0,2,1:T(8,128)S(1)} %get-tuple-element.74, f32[128,4,1018]{0,2,1:T(8,128)S(1)} %get-tuple-element.76, f32[128,4,1018]{0,2,1:T(8,128)S(1)} %get-tuple-element.75, f32[128,4,6]{0,2,1:T(8,128)S(1)} %get-tuple-element.73, f32[128,4,6]{0,2,1:T(8,128)S(1)} %get-tuple-element.70, ...), kind=kLoop, calls=%fused_computation.76 | loop fusion | flops 45088768 | bytes 50345472 | tf_op jit(solution)/shard_map/add | solution.py:74
  335.9 2.0 copy.47
  337.9 1.6 copy.57
  339.5 1.7 copy.46
  (277 shorter events, 17.3 us)
Async XLA Ops:
  7.2 98.4 %copy-start = (bf16[4,128,256]{2,1,0:T(8,128)(2,1)S(1)}, bf16[4,128,256]{2,1,0:T(8,128)(2,1)}, u32[]{:S(2)}) copy-start(bf16[4,128,256]{2,1,0:T(8,128)(2,1)} %param.6) | copy-start | bytes 786436
  7.2 98.4 %all-gather.2.cloned.1.call-start = ((), (), s32[]{:S(2)}) async-start(), calls=%async_computation.1 | async-start | bytes 3145728 | tf_op jit(solution)/shard_map/all_gather | solution.py:58
  9.2 15.7 %copy-start.56 = (bf16[128,4,1024]{2,1,0:T(4,128)(2,1)S(1)}, bf16[128,4,1024]{2,1,0:T(4,128)(2,1)}, u32[]{:S(2)}) copy-start(bf16[128,4,1024]{2,1,0:T(4,128)(2,1)} %param.7) | copy-start | bytes 3145732
  10.2 34.8 %collective-permute-start.8 = (bf16[128,2,1024]{0,2,1:T(8,128)(2,1)}, bf16[128,2,1024]{0,2,1:T(8,128)(2,1)S(1)}, u32[]{:S(2)}, u32[]{:S(2)}) collective-permute-start(bf16[128,2,1024]{0,2,1:T(8,128)(2,1)} %get-tuple-element.125), channel_id=1, source_target_pairs={{8,0},{10,2},{12,4},{14,6},{16,8},{18,10},{20,12},{22,14},{24,16},... | collective-permute-start | bytes 1572872 | tf_op jit(solution)/shard_map/ppermute | solution.py:15
  11.5 21.3 %collective-permute-start.6 = (bf16[128,2,1024]{0,2,1:T(8,128)(2,1)}, bf16[128,2,1024]{0,2,1:T(8,128)(2,1)S(1)}, u32[]{:S(2)}, u32[]{:S(2)}) collective-permute-start(bf16[128,2,1024]{0,2,1:T(8,128)(2,1)} %get-tuple-element.125), channel_id=1, source_target_pairs={{0,10},{2,12},{4,14},{6,16},{8,18},{10,20},{12,22},{14,24},{16,26}... | collective-permute-start | bytes 1572872 | tf_op jit(solution)/shard_map/ppermute | solution.py:15
  16.6 33.8 %collective-permute-start.2 = (bf16[128,2,1024]{0,2,1:T(8,128)(2,1)}, bf16[128,2,1024]{0,2,1:T(8,128)(2,1)}, u32[]{:S(2)}, u32[]{:S(2)}) collective-permute-start(bf16[128,2,1024]{0,2,1:T(8,128)(2,1)} %get-tuple-element.125), channel_id=1, source_target_pairs={{2,0},{4,2},{6,4},{8,6},{10,8},{12,10},{14,12},{16,14},{18,16},{20... | collective-permute-start | bytes 1572872 | tf_op jit(solution)/shard_map/ppermute | solution.py:15
  17.9 53.2 %collective-permute-start = (bf16[128,2,1024]{0,2,1:T(8,128)(2,1)}, bf16[128,2,1024]{0,2,1:T(8,128)(2,1)}, u32[]{:S(2)}, u32[]{:S(2)}) collective-permute-start(bf16[128,2,1024]{0,2,1:T(8,128)(2,1)} %get-tuple-element.125), channel_id=1, source_target_pairs={{0,4},{2,6},{4,8},{6,10},{8,12},{10,14},{12,16},{14,18},{16,20},{1... | collective-permute-start | bytes 1572872 | tf_op jit(solution)/shard_map/ppermute | solution.py:15
  26.3 233.1 %all-reduce.2.cloned.1.call-start = ((), (), s32[]{:S(2)}) async-start(), calls=%async_computation.2 | async-start | bytes 1081344 | tf_op jit(solution)/shard_map/psum | solution.py:86
  26.3 14.9 %collective-permute-start.7 = (bf16[128,2,1024]{0,2,1:T(8,128)(2,1)}, bf16[128,2,1024]{0,2,1:T(8,128)(2,1)S(1)}, u32[]{:S(2)}, u32[]{:S(2)}) collective-permute-start(bf16[128,2,1024]{0,2,1:T(8,128)(2,1)} %get-tuple-element.126), channel_id=1, source_target_pairs={{0,8},{2,10},{4,12},{6,14},{8,16},{10,18},{12,20},{14,22},{16,24},... | collective-permute-start | bytes 1572872 | tf_op jit(solution)/shard_map/ppermute | solution.py:15
  29.0 52.9 %copy-start.74 = (f32[128,4,6]{0,2,1:T(8,128)}, f32[128,4,6]{0,2,1:T(8,128)S(1)}, u32[]{:S(2)}) copy-start(f32[128,4,6]{0,2,1:T(8,128)S(1)} %get-tuple-element.105) | copy-start | bytes 36868
  29.0 52.9 %copy-start.76 = (f32[128,4,6]{0,2,1:T(8,128)}, f32[128,4,6]{0,2,1:T(8,128)S(1)}, u32[]{:S(2)}) copy-start(f32[128,4,6]{0,2,1:T(8,128)S(1)} %get-tuple-element.106) | copy-start | bytes 36868
  29.1 70.9 %copy-start.62 = (f32[128,4,12]{0,2,1:T(8,128)}, f32[128,4,12]{0,2,1:T(8,128)S(1)}, u32[]{:S(2)}) copy-start(f32[128,4,12]{0,2,1:T(8,128)S(1)} %get-tuple-element.113) | copy-start | bytes 73732
  29.1 70.9 %copy-start.64 = (f32[128,4,12]{0,2,1:T(8,128)}, f32[128,4,12]{0,2,1:T(8,128)S(1)}, u32[]{:S(2)}) copy-start(f32[128,4,12]{0,2,1:T(8,128)S(1)} %get-tuple-element.114) | copy-start | bytes 73732
  29.4 44.5 %copy-start.24 = (f32[128,4,1006]{0,2,1:T(8,128)}, f32[128,4,1006]{0,2,1:T(8,128)S(1)}, u32[]{:S(2)}) copy-start(f32[128,4,1006]{0,2,1:T(8,128)S(1)} %get-tuple-element.123) | copy-start | bytes 6180868
  29.4 44.5 %copy-start.25 = (f32[128,4,1006]{0,2,1:T(8,128)}, f32[128,4,1006]{0,2,1:T(8,128)S(1)}, u32[]{:S(2)}) copy-start(f32[128,4,1006]{0,2,1:T(8,128)S(1)} %get-tuple-element.124) | copy-start | bytes 6180868
  30.1 69.8 %copy-start.16 = (f32[128,4,1012]{0,2,1:T(8,128)}, f32[128,4,1012]{0,2,1:T(8,128)S(1)}, u32[]{:S(2)}) copy-start(f32[128,4,1012]{0,2,1:T(8,128)S(1)} %get-tuple-element.115) | copy-start | bytes 6217732
  30.1 69.8 %copy-start.18 = (f32[128,4,1012]{0,2,1:T(8,128)}, f32[128,4,1012]{0,2,1:T(8,128)S(1)}, u32[]{:S(2)}) copy-start(f32[128,4,1012]{0,2,1:T(8,128)S(1)} %get-tuple-element.116) | copy-start | bytes 6217732
  31.4 42.5 %copy-start.88 = (f32[128]{0:T(128)}, f32[128]{0:T(128)S(1)}, u32[]{:S(2)}) copy-start(f32[128]{0:T(128)S(1)} %get-tuple-element.128) | copy-start | bytes 1540
  31.4 42.6 %copy-start.89 = (f32[128]{0:T(128)}, f32[128]{0:T(128)S(1)}, u32[]{:S(2)}) copy-start(f32[128]{0:T(128)S(1)} %get-tuple-element.129) | copy-start | bytes 1540
  31.4 42.6 %copy-start.90 = (f32[128]{0:T(128)}, f32[128]{0:T(128)S(1)}, u32[]{:S(2)}) copy-start(f32[128]{0:T(128)S(1)} %get-tuple-element.130) | copy-start | bytes 1540
  31.4 42.6 %copy-start.91 = (f32[128]{0:T(128)}, f32[128]{0:T(128)S(1)}, u32[]{:S(2)}) copy-start(f32[128]{0:T(128)S(1)} %get-tuple-element.131) | copy-start | bytes 1540
  31.4 42.6 %copy-start.92 = (f32[128]{0:T(128)}, f32[128]{0:T(128)S(1)}, u32[]{:S(2)}) copy-start(f32[128]{0:T(128)S(1)} %get-tuple-element.132) | copy-start | bytes 1540
  31.4 42.6 %copy-start.93 = (f32[128]{0:T(128)}, f32[128]{0:T(128)S(1)}, u32[]{:S(2)}) copy-start(f32[128]{0:T(128)S(1)} %get-tuple-element.133) | copy-start | bytes 1540
  31.4 42.6 %copy-start.94 = (f32[128]{0:T(128)}, f32[128]{0:T(128)S(1)}, u32[]{:S(2)}) copy-start(f32[128]{0:T(128)S(1)} %get-tuple-element.134) | copy-start | bytes 1540
  31.4 42.6 %copy-start.95 = (f32[128]{0:T(128)}, f32[128]{0:T(128)S(1)}, u32[]{:S(2)}) copy-start(f32[128]{0:T(128)S(1)} %get-tuple-element.135) | copy-start | bytes 1540
  31.4 42.6 %copy-start.96 = (f32[128]{0:T(128)}, f32[128]{0:T(128)S(1)}, u32[]{:S(2)}) copy-start(f32[128]{0:T(128)S(1)} %get-tuple-element.136) | copy-start | bytes 1540
  31.4 50.5 %copy-start.86 = (f32[128]{0:T(128)}, f32[128]{0:T(128)S(1)}, u32[]{:S(2)}) copy-start(f32[128]{0:T(128)S(1)} %get-tuple-element.127) | copy-start | bytes 1540
  32.8 49.2 %copy-start.4 = (f32[128,4,1018]{0,2,1:T(8,128)}, f32[128,4,1018]{0,2,1:T(8,128)S(1)}, u32[]{:S(2)}) copy-start(f32[128,4,1018]{0,2,1:T(8,128)S(1)} %get-tuple-element.107) | copy-start | bytes 6254596
  32.8 49.2 %copy-start.6 = (f32[128,4,1018]{0,2,1:T(8,128)}, f32[128,4,1018]{0,2,1:T(8,128)S(1)}, u32[]{:S(2)}) copy-start(f32[128,4,1018]{0,2,1:T(8,128)S(1)} %get-tuple-element.108) | copy-start | bytes 6254596
  32.8 12.2 %copy-start.32 = (bf16[128,2,1024]{0,2,1:T(8,128)(2,1)}, bf16[128,2,1024]{0,2,1:T(8,128)(2,1)S(1)}, u32[]{:S(2)}) copy-start(bf16[128,2,1024]{0,2,1:T(8,128)(2,1)S(1)} %collective-permute-done.6) | copy-start | bytes 1572868
  32.8 13.9 %collective-permute-start.9 = (bf16[128,2,1024]{0,2,1:T(8,128)(2,1)}, bf16[128,2,1024]{0,2,1:T(8,128)(2,1)S(1)}, u32[]{:S(2)}, u32[]{:S(2)}) collective-permute-start(bf16[128,2,1024]{0,2,1:T(8,128)(2,1)} %get-tuple-element.126), channel_id=1, source_target_pairs={{10,0},{12,2},{14,4},{16,6},{18,8},{20,10},{22,12},{24,14},{26,16}... | collective-permute-start | bytes 1572872 | tf_op jit(solution)/shard_map/ppermute | solution.py:15
  41.2 32.8 %copy-start.35 = (bf16[128,2,1024]{0,2,1:T(8,128)(2,1)}, bf16[128,2,1024]{0,2,1:T(8,128)(2,1)S(1)}, u32[]{:S(2)}) copy-start(bf16[128,2,1024]{0,2,1:T(8,128)(2,1)S(1)} %collective-permute-done.7) | copy-start | bytes 1572868
  41.2 28.2 %collective-permute-start.3 = (bf16[128,2,1024]{0,2,1:T(8,128)(2,1)}, bf16[128,2,1024]{0,2,1:T(8,128)(2,1)S(1)}, u32[]{:S(2)}, u32[]{:S(2)}) collective-permute-start(bf16[128,2,1024]{0,2,1:T(8,128)(2,1)} %get-tuple-element.126), channel_id=1, source_target_pairs={{4,0},{6,2},{8,4},{10,6},{12,8},{14,10},{16,12},{18,14},{20,16},{2... | collective-permute-start | bytes 1572872 | tf_op jit(solution)/shard_map/ppermute | solution.py:15
  42.7 31.3 %copy-start.58 = (f32[128,4,18]{0,2,1:T(8,128)}, f32[128,4,18]{0,2,1:T(8,128)S(1)}, u32[]{:S(2)}) copy-start(f32[128,4,18]{0,2,1:T(8,128)S(1)} %get-tuple-element.85) | copy-start | bytes 110596
  42.7 31.3 %copy-start.60 = (f32[128,4,18]{0,2,1:T(8,128)}, f32[128,4,18]{0,2,1:T(8,128)S(1)}, u32[]{:S(2)}) copy-start(f32[128,4,18]{0,2,1:T(8,128)S(1)} %get-tuple-element.86) | copy-start | bytes 110596
  45.0 26.1 %collective-permute-start.1 = (bf16[128,2,1024]{0,2,1:T(8,128)(2,1)}, bf16[128,2,1024]{0,2,1:T(8,128)(2,1)S(1)}, u32[]{:S(2)}, u32[]{:S(2)}) collective-permute-start(bf16[128,2,1024]{0,2,1:T(8,128)(2,1)} %get-tuple-element.126), channel_id=1, source_target_pairs={{0,2},{2,4},{4,6},{6,8},{8,10},{10,12},{12,14},{14,16},{16,18},{18... | collective-permute-start | bytes 1572872 | tf_op jit(solution)/shard_map/ppermute | solution.py:15
  46.7 41.2 %collective-permute-start.5 = (bf16[128,4,1024]{0,2,1:T(8,128)(2,1)S(1)}, bf16[128,4,1024]{0,2,1:T(8,128)(2,1)S(1)}, u32[]{:S(2)}, u32[]{:S(2)}) collective-permute-start(bf16[128,4,1024]{0,2,1:T(8,128)(2,1)S(1)} %copy.35), channel_id=1, source_target_pairs={{6,0},{8,2},{10,4},{12,6},{14,8},{16,10},{18,12},{20,14},{22,16},{... | collective-permute-start | bytes 3145736 | tf_op jit(solution)/shard_map/ppermute | solution.py:15
  48.2 25.9 %copy-start.57 = (f32[128,4,18]{0,2,1:T(8,128)}, f32[128,4,18]{0,2,1:T(8,128)S(1)}, u32[]{:S(2)}) copy-start(f32[128,4,18]{0,2,1:T(8,128)S(1)} %get-tuple-element.90) | copy-start | bytes 110596
  50.4 47.1 %collective-permute-start.4 = (bf16[128,4,1024]{0,2,1:T(8,128)(2,1)S(1)}, bf16[128,4,1024]{0,2,1:T(8,128)(2,1)S(1)}, u32[]{:S(2)}, u32[]{:S(2)}) collective-permute-start(bf16[128,4,1024]{0,2,1:T(8,128)(2,1)S(1)} %copy.35), channel_id=1, source_target_pairs={{0,6},{2,8},{4,10},{6,12},{8,14},{10,16},{12,18},{14,20},{16,22},{... | collective-permute-start | bytes 3145736 | tf_op jit(solution)/shard_map/ppermute | solution.py:15
  71.1 10.9 %copy-start.12 = (f32[128,4,1018]{0,2,1:T(8,128)}, f32[128,4,1018]{0,2,1:T(8,128)S(1)}, u32[]{:S(2)}) copy-start(f32[128,4,1018]{0,2,1:T(8,128)S(1)} %get-tuple-element.84) | copy-start | bytes 6254596
  71.1 10.9 %copy-start.14 = (f32[128,4,1018]{0,2,1:T(8,128)}, f32[128,4,1018]{0,2,1:T(8,128)S(1)}, u32[]{:S(2)}) copy-start(f32[128,4,1018]{0,2,1:T(8,128)S(1)} %get-tuple-element.83) | copy-start | bytes 6254596
  73.9 8.1 %copy-start.8 = (f32[128,4,1018]{0,2,1:T(8,128)}, f32[128,4,1018]{0,2,1:T(8,128)S(1)}, u32[]{:S(2)}) copy-start(f32[128,4,1018]{0,2,1:T(8,128)S(1)} %get-tuple-element.79) | copy-start | bytes 6254596
  73.9 8.1 %copy-start.10 = (f32[128,4,1018]{0,2,1:T(8,128)}, f32[128,4,1018]{0,2,1:T(8,128)S(1)}, u32[]{:S(2)}) copy-start(f32[128,4,1018]{0,2,1:T(8,128)S(1)} %get-tuple-element.80) | copy-start | bytes 6254596
  81.9 6.0 %copy-start.79 = (f32[128,4,6]{0,2,1:T(8,128)}, f32[128,4,6]{0,2,1:T(8,128)S(1)}, u32[]{:S(2)}) copy-start(f32[128,4,6]{0,2,1:T(8,128)S(1)} %get-tuple-element.77) | copy-start | bytes 36868
  81.9 6.0 %copy-start.81 = (f32[128,4,6]{0,2,1:T(8,128)}, f32[128,4,6]{0,2,1:T(8,128)S(1)}, u32[]{:S(2)}) copy-start(f32[128,4,6]{0,2,1:T(8,128)S(1)} %get-tuple-element.78) | copy-start | bytes 36868
  87.9 12.1 %copy-start.66 = (f32[128,4,12]{0,2,1:T(8,128)}, f32[128,4,12]{0,2,1:T(8,128)S(1)}, u32[]{:S(2)}) copy-start(f32[128,4,12]{0,2,1:T(8,128)S(1)} %get-tuple-element.118) | copy-start | bytes 73732
  87.9 12.1 %copy-start.68 = (f32[128,4,12]{0,2,1:T(8,128)}, f32[128,4,12]{0,2,1:T(8,128)S(1)}, u32[]{:S(2)}) copy-start(f32[128,4,12]{0,2,1:T(8,128)S(1)} %get-tuple-element.117) | copy-start | bytes 73732
  109.1 13.9 %copy-start.2 = (bf16[4,128,4,1024]{1,3,2,0:T(8,128)(2,1)}, bf16[4,128,4,1024]{1,3,2,0:T(8,128)(2,1)S(1)}, u32[]{:S(2)}) copy-start(bf16[4,128,4,1024]{1,3,2,0:T(8,128)(2,1)S(1)} %convolution_convert_fusion) | copy-start | bytes 12582916
  123.1 7.4 %copy-start.13 = (f32[128,4,1018]{0,2,1:T(8,128)S(1)}, f32[128,4,1018]{0,2,1:T(8,128)}, u32[]{:S(2)}) copy-start(f32[128,4,1018]{0,2,1:T(8,128)} %copy-done.12) | copy-start | bytes 6254596
  142.3 195.6 %reduce-scatter.4.cloned.1.call-start = ((), (), s32[]{:S(2)}) async-start(), calls=%async_computation.3 | async-start | bytes 3145728
  153.5 116.2 %collective-permute-start.18 = (bf16[128,2,1024]{0,2,1:T(8,128)(2,1)}, bf16[128,2,1024]{0,2,1:T(8,128)(2,1)S(1)}, u32[]{:S(2)}, u32[]{:S(2)}) collective-permute-start(bf16[128,2,1024]{0,2,1:T(8,128)(2,1)} %get-tuple-element.93), channel_id=1, source_target_pairs={{0,10},{2,12},{4,14},{6,16},{8,18},{10,20},{12,22},{14,24},{16,26}... | collective-permute-start | bytes 1572872 | tf_op jit(solution)/shard_map/ppermute | solution.py:15
  173.7 89.1 %collective-permute-start.16 = (bf16[128,2,1024]{0,2,1:T(8,128)(2,1)}, bf16[128,2,1024]{0,2,1:T(8,128)(2,1)S(1)}, u32[]{:S(2)}, u32[]{:S(2)}) collective-permute-start(bf16[128,2,1024]{0,2,1:T(8,128)(2,1)} %get-tuple-element.93), channel_id=1, source_target_pairs={{8,0},{10,2},{12,4},{14,6},{16,8},{18,10},{20,12},{22,14},{24,16},... | collective-permute-start | bytes 1572872 | tf_op jit(solution)/shard_map/ppermute | solution.py:15
  175.0 96.0 %collective-permute-start.19 = (bf16[128,2,1024]{0,2,1:T(8,128)(2,1)}, bf16[128,2,1024]{0,2,1:T(8,128)(2,1)S(1)}, u32[]{:S(2)}, u32[]{:S(2)}) collective-permute-start(bf16[128,2,1024]{0,2,1:T(8,128)(2,1)} %get-tuple-element.94), channel_id=1, source_target_pairs={{0,8},{2,10},{4,12},{6,14},{8,16},{10,18},{12,20},{14,22},{16,24},... | collective-permute-start | bytes 1572872 | tf_op jit(solution)/shard_map/ppermute | solution.py:15
  180.6 83.5 %collective-permute-start.17 = (bf16[128,2,1024]{0,2,1:T(8,128)(2,1)}, bf16[128,2,1024]{0,2,1:T(8,128)(2,1)S(1)}, u32[]{:S(2)}, u32[]{:S(2)}) collective-permute-start(bf16[128,2,1024]{0,2,1:T(8,128)(2,1)} %get-tuple-element.94), channel_id=1, source_target_pairs={{10,0},{12,2},{14,4},{16,6},{18,8},{20,10},{22,12},{24,14},{26,16}... | collective-permute-start | bytes 1572872 | tf_op jit(solution)/shard_map/ppermute | solution.py:15
  190.0 95.7 %collective-permute-start.12 = (bf16[128,2,1024]{0,2,1:T(8,128)(2,1)}, bf16[128,2,1024]{0,2,1:T(8,128)(2,1)}, u32[]{:S(2)}, u32[]{:S(2)}) collective-permute-start(bf16[128,2,1024]{0,2,1:T(8,128)(2,1)} %get-tuple-element.103), channel_id=1, source_target_pairs={{0,4},{2,6},{4,8},{6,10},{8,12},{10,14},{12,16},{14,18},{16,20},{1... | collective-permute-start | bytes 1572872 | tf_op jit(solution)/shard_map/ppermute | solution.py:15
  262.8 6.9 %copy-start.44 = (bf16[128,2,1024]{0,2,1:T(8,128)(2,1)}, bf16[128,2,1024]{0,2,1:T(8,128)(2,1)S(1)}, u32[]{:S(2)}) copy-start(bf16[128,2,1024]{0,2,1:T(8,128)(2,1)S(1)} %collective-permute-done.16) | copy-start | bytes 1572868
  262.8 16.6 %collective-permute-start.10 = (bf16[128,2,1024]{0,2,1:T(8,128)(2,1)}, bf16[128,2,1024]{0,2,1:T(8,128)(2,1)S(1)}, u32[]{:S(2)}, u32[]{:S(2)}) collective-permute-start(bf16[128,2,1024]{0,2,1:T(8,128)(2,1)} %get-tuple-element.103), channel_id=1, source_target_pairs={{2,0},{4,2},{6,4},{8,6},{10,8},{12,10},{14,12},{16,14},{18,16},{20... | collective-permute-start | bytes 1572872 | tf_op jit(solution)/shard_map/ppermute | solution.py:15
  264.1 21.6 %collective-permute-start.13 = (bf16[128,2,1024]{0,2,1:T(8,128)(2,1)}, bf16[128,2,1024]{0,2,1:T(8,128)(2,1)S(1)}, u32[]{:S(2)}, u32[]{:S(2)}) collective-permute-start(bf16[128,2,1024]{0,2,1:T(8,128)(2,1)} %get-tuple-element.104), channel_id=1, source_target_pairs={{0,2},{2,4},{4,6},{6,8},{8,10},{10,12},{12,14},{14,16},{16,18},{18... | collective-permute-start | bytes 1572872 | tf_op jit(solution)/shard_map/ppermute | solution.py:15
  269.7 9.7 %copy-start.42 = (bf16[128,2,1024]{0,2,1:T(8,128)(2,1)}, bf16[128,2,1024]{0,2,1:T(8,128)(2,1)S(1)}, u32[]{:S(2)}) copy-start(bf16[128,2,1024]{0,2,1:T(8,128)(2,1)S(1)} %collective-permute-done.18) | copy-start | bytes 1572868
  269.7 15.8 %collective-permute-start.11 = (bf16[128,2,1024]{0,2,1:T(8,128)(2,1)}, bf16[128,2,1024]{0,2,1:T(8,128)(2,1)S(1)}, u32[]{:S(2)}, u32[]{:S(2)}) collective-permute-start(bf16[128,2,1024]{0,2,1:T(8,128)(2,1)} %get-tuple-element.104), channel_id=1, source_target_pairs={{4,0},{6,2},{8,4},{10,6},{12,8},{14,10},{16,12},{18,14},{20,16},{2... | collective-permute-start | bytes 1572872 | tf_op jit(solution)/shard_map/ppermute | solution.py:15
  271.0 8.4 %copy-start.46 = (bf16[128,2,1024]{0,2,1:T(8,128)(2,1)}, bf16[128,2,1024]{0,2,1:T(8,128)(2,1)S(1)}, u32[]{:S(2)}) copy-start(bf16[128,2,1024]{0,2,1:T(8,128)(2,1)S(1)} %collective-permute-done.19) | copy-start | bytes 1572868
  271.0 42.1 %collective-permute-start.15 = (bf16[128,4,1024]{0,2,1:T(8,128)(2,1)S(1)}, bf16[128,4,1024]{0,2,1:T(8,128)(2,1)S(1)}, u32[]{:S(2)}, u32[]{:S(2)}) collective-permute-start(bf16[128,4,1024]{0,2,1:T(8,128)(2,1)S(1)} %copy-done.54), channel_id=1, source_target_pairs={{0,6},{2,8},{4,10},{6,12},{8,14},{10,16},{12,18},{14,20},{16,22},{... | collective-permute-start | bytes 3145736 | tf_op jit(solution)/shard_map/ppermute | solution.py:15
  279.4 7.7 %copy-start.48 = (bf16[128,2,1024]{0,2,1:T(8,128)(2,1)}, bf16[128,2,1024]{0,2,1:T(8,128)(2,1)S(1)}, u32[]{:S(2)}) copy-start(bf16[128,2,1024]{0,2,1:T(8,128)(2,1)S(1)} %collective-permute-done.10) | copy-start | bytes 1572868
  279.4 33.7 %collective-permute-start.14 = (bf16[128,4,1024]{0,2,1:T(8,128)(2,1)S(1)}, bf16[128,4,1024]{0,2,1:T(8,128)(2,1)S(1)}, u32[]{:S(2)}, u32[]{:S(2)}) collective-permute-start(bf16[128,4,1024]{0,2,1:T(8,128)(2,1)S(1)} %copy-done.54), channel_id=1, source_target_pairs={{6,0},{8,2},{10,4},{12,6},{14,8},{16,10},{18,12},{20,14},{22,16},{... | collective-permute-start | bytes 3145736 | tf_op jit(solution)/shard_map/ppermute | solution.py:15
  (65 other events, 237.4 us)
Sparse Core Ops, SparseCore 0:
  26.4 32.4 all-gather.1
  142.4 116.8 all-reduce.1
  261.6 32.2 reduce-scatter.3
where the time goes:
time: 349 us; the launch traced here: 348 us
  waiting for transfers between devices  113 us (32%)
  starting transfers between devices  86.2 us (25%)
  other arithmetic  67.8 us (19%)
  local copies, waits for them, and re-layouts  58 us (17%)
  between operations  15.4 us (4%)
  matrix products  7.47 us (2%)
    ppermute x20, starting transfers between devices, shifted(): return lax.ppermute(block, axis, route)  86.1 us
    psum x1, waiting for transfers between devices, local(): flat = lax.psum(flat, 'band')  66.5 us
    ppermute x20, waiting for transfers between devices, shifted(): return lax.ppermute(block, axis, route)  46.3 us
    reduce_sum x4, other arithmetic, local(): jnp.sum(grad_f * jnp.roll(feat_rows[row_step * spacing], -col_step * spac...  21.7 us
    unnamed x220, local copies, waits for them, and re-layouts  20.7 us
    slice x18, local copies, waits for them, and re-layouts, local(): jnp.roll(grad_rows[-row_step * spacing], col_step * spacing, axis=-1)  17.5 us
    another operation x3, other arithmetic, local(): stacked = jnp.stack(branches)  17.2 us
    add x1, other arithmetic, local(): grad_input + kernel[which, tap_index][:, None, None] * jnp.roll(grad_rows...  15.6 us
  transfers between devices with their start and end apart: 23, of which 5 were waited for; matrix products, arithmetic and copies ran while one was open for 24% of the time, Pallas kernels for 0%

commit v1 on v0

--- a/solution.py
+++ b/solution.py
@@ -83,7 +83,7 @@
         depth_rows.append(jnp.stack(tap_rows))
     depth_local = jnp.stack(depth_rows)
     flat = jnp.concatenate([depth_local.reshape(-1), point_local.reshape(-1)])
-    flat = lax.psum(flat, "band")
+    flat = jnp.sum(lax.all_gather(flat, "band"), axis=0)
     depth_total = flat[: depth_local.size].reshape(depth_local.shape)
     point_total = flat[depth_local.size :].reshape(point_local.shape)
     return (output, grad_input, depth_total / GSCALE, point_total / GSCALE)

time: 349 us -> 366 us (1.049)
  the two profiles are of different devices: /device:TPU:0 before, /device:TPU:18 now
where the time goes in v1:
time: 366 us; the launch traced here: 365 us
  waiting for transfers between devices  112 us (31%)
  other arithmetic  97.2 us (27%)
  starting transfers between devices  78.2 us (21%)
  local copies, waits for them, and re-layouts  54.1 us (15%)
  between operations  15.8 us (4%)
  matrix products  7.72 us (2%)
    ppermute x20, waiting for transfers between devices, shifted(): return lax.ppermute(block, axis, route)  112 us
    ppermute x20, starting transfers between devices, shifted(): return lax.ppermute(block, axis, route)  77.9 us
    reduce_sum x1, other arithmetic, local(): flat = jnp.sum(lax.all_gather(flat, 'band'), axis=0)  41.2 us
    unnamed x251, local copies, waits for them, and re-layouts  29.4 us
    reduce_sum x4, other arithmetic, local(): jnp.sum(grad_f * jnp.roll(feat_rows[row_step * spacing], -col_step * spac...  17.3 us
    add x1, other arithmetic, local(): grad_input + kernel[which, tap_index][:, None, None] * jnp.roll(grad_rows...  15.8 us
    another operation x3, other arithmetic, local(): stacked = jnp.stack(branches)  14.5 us
    slice x18, local copies, waits for them, and re-layouts, local(): jnp.roll(grad_rows[-row_step * spacing], col_step * spacing, axis=-1)  13.9 us
  transfers between devices with their start and end apart: 23, of which 8 were waited for; matrix products, arithmetic and copies ran while one was open for 28% of the time, Pallas kernels for 0%

profile of v1, /device:TPU:18, one launch (start us, length us, event | category | flops | bytes accessed | tf_op | source)
XLA Modules:
  0.0 364.7 jit_solution(14777609560756283929)
XLA Ops:
  7.2 2.0 copy.35
  9.3 1.0 fusion.123
  10.3 2.3 collective-permute-start.8
  12.7 3.5 collective-permute-start.6
  16.1 3.9 %collective-permute-start.2 = (bf16[128,2,1024]{0,2,1:T(8,128)(2,1)}, bf16[128,2,1024]{0,2,1:T(8,128)(2,1)}, u32[]{:S(2)}, u32[]{:S(2)}) collective-permute-start(bf16[128,2,1024]{0,2,1:T(8,128)(2,1)} %get-tuple-element.125), channel_id=1, source_target_pairs={{2,0},{4,2},{6,4},{8,6},{10,8},{12,10},{14,12},{16,14},{18,16},{20... | collective-permute-start | bytes 1572872 | tf_op jit(solution)/shard_map/ppermute | solution.py:15
  20.1 1.9 collective-permute-start
  22.0 1.4 copy.43
  23.5 1.9 collective-permute-start.7
  26.5 1.1 slice_bitcast_fusion.30
  27.7 1.0 slice_bitcast_fusion.29
  29.0 1.4 collective-permute-done.6
  30.4 1.9 collective-permute-start.9
  32.3 27.8 %collective-permute-done.7 = bf16[128,2,1024]{0,2,1:T(8,128)(2,1)S(1)} collective-permute-done((bf16[128,2,1024]{0,2,1:T(8,128)(2,1)}, bf16[128,2,1024]{0,2,1:T(8,128)(2,1)S(1)}, u32[]{:S(2)}, u32[]{:S(2)}) %collective-permute-start.7) | collective-permute-done | bytes 524320 | tf_op jit(solution)/shard_map/ppermute | solution.py:15
  60.1 1.9 collective-permute-start.3
  62.0 1.2 maximum_convert_fusion.2
  63.3 2.3 fusion.104
  65.6 3.3 collective-permute-start.1
  68.9 2.8 collective-permute-start.5
  71.7 1.2 maximum_convert_fusion.3
  72.9 2.3 fusion.106
  75.2 3.9 %collective-permute-start.4 = (bf16[128,4,1024]{0,2,1:T(8,128)(2,1)S(1)}, bf16[128,4,1024]{0,2,1:T(8,128)(2,1)S(1)}, u32[]{:S(2)}, u32[]{:S(2)}) collective-permute-start(bf16[128,4,1024]{0,2,1:T(8,128)(2,1)S(1)} %copy.35), channel_id=1, source_target_pairs={{0,6},{2,8},{4,10},{6,12},{8,14},{10,16},{12,18},{14,20},{16,22},{... | collective-permute-start | bytes 3145736 | tf_op jit(solution)/shard_map/ppermute | solution.py:15
  79.7 1.4 maximum_convert_fusion.1
  81.4 14.9 %collective-permute-done.1 = bf16[128,2,1024]{0,2,1:T(8,128)(2,1)S(1)} collective-permute-done((bf16[128,2,1024]{0,2,1:T(8,128)(2,1)}, bf16[128,2,1024]{0,2,1:T(8,128)(2,1)S(1)}, u32[]{:S(2)}, u32[]{:S(2)}) %collective-permute-start.1) | collective-permute-done | bytes 524320 | tf_op jit(solution)/shard_map/ppermute | solution.py:15
  97.1 1.2 maximum_convert_fusion
  99.3 7.3 %fusion.75 = bf16[1,128,4,1024]{1,3,0,2:T(8,128)(2,1)} fusion(f32[128,4,18]{0,2,1:T(8,128)S(1)} %get-tuple-element.90, f32[128,4,1006]{0,2,1:T(8,128)} %get-tuple-element.92, f32[128]{0:T(128)S(1)} %get-tuple-element.128, f32[128]{0:T(128)S(1)} %get-tuple-element.129, f32[128,4,1006]{0,2,1:T(8,128)} %get-tuple-element.91, ...), kind=kLoop, calls=%fused_computation.159 | loop fusion | flops 15204352 | bytes 16781824 | tf_op jit(solution)/shard_map/stack | solution.py:49
  106.7 5.0 %fusion.77 = bf16[1,128,4,1024]{1,3,0,2:T(8,128)(2,1)S(1)} fusion(f32[128,4,6]{0,2,1:T(8,128)S(1)} %get-tuple-element.82, f32[128,4,1018]{0,2,1:T(8,128)S(1)} %get-tuple-element.84, f32[128]{0:T(128)} %get-tuple-element.147, f32[128]{0:T(128)} %get-tuple-element.148, f32[128,4,1018]{0,2,1:T(8,128)S(1)} %get-tuple-element.83, ...), kind=kLoop, calls=%fused_computation.161 | loop fusion | flops 15204352 | bytes 16781824 | tf_op jit(solution)/shard_map/stack | solution.py:49
  114.3 2.2 fusion.76
  116.6 2.4 bitcast_convert_fusion
  119.1 4.1 %copy.56 = bf16[256,4096]{1,0:T(8,128)(2,1)} copy(bf16[256,4096]{0,1:T(8,128)(2,1)} %bitcast.200) | data formatting | bytes 4194304
  123.5 4.0 %fusion.72 = f32[4,128,256,1]{2,1,0,3:T(8,128)S(1)} fusion(bf16[256,4,1024]{2,0,1:T(8,128)(2,1)} %all-gather.5.cloned.1.call-done, bf16[1,128,4,1024]{1,3,0,2:T(8,128)(2,1)} %fusion.75, bf16[1,128,4,1024]{1,3,0,2:T(8,128)(2,1)} %copy-done.54, bf16[1,128,4,1024]{1,3,0,2:T(8,128)(2,1)} %copy-done.53, bf16[1,128,4,1024]{1,3,0,2:T(8,128)(2,1)S(1)} %bitcast.198), kind=kOutput, calls=%fused_computation.144 | convolution fusion | flops 1080033280 | bytes 6815744 | tf_op jit(solution)/shard_map/bchw,ohw->bco/dot_general | solution.py:60
  127.5 1.1 copy.58
  128.7 1.3 convolution_convert_fusion
  132.3 2.4 fusion.47
  137.3 4.7 %fusion.45 = (f32[128]{0:T(128)}, f32[128]{0:T(128)}, f32[128]{0:T(128)}, f32[128]{0:T(128)}, f32[128]{0:T(128)}, /*index=5*/f32[128]{0:T(128)}, f32[128]{0:T(128)}, f32[128]{0:T(128)}) fusion(bf16[128,4,1024]{0,2,1:T(8,128)(2,1)S(1)} %copy.35, bf16[4,128,4,1024]{1,3,2,0:T(8,128)(2,1)S(1)} %convolution_convert_fusion, f32[128,4,6]{0,2,1:T(8,128)S(1)} %copy-done.77, ...), kind=kLoop, calls=%fused_computation.81 | loop fusion | flops 13630464 | bytes 13635584 | tf_op jit(solution)/shard_map/reduce_sum | solution.py:78
  142.2 3.8 %fusion.48 = (f32[128]{0:T(128)S(1)}, f32[128]{0:T(128)S(1)}, f32[128]{0:T(128)S(1)}, f32[128]{0:T(128)S(1)}, f32[128]{0:T(128)S(1)}, /*index=5*/f32[128]{0:T(128)S(1)}, f32[128]{0:T(128)S(1)}) fusion(bf16[128,2,1024]{0,2,1:T(8,128)(2,1)S(1)} %copy-done.39, bf16[128,2,1024]{0,2,1:T(8,128)(2,1)} %collective-permute-done.2, ...), kind=kLoop, calls=%fused_computation.84 | loop fusion | flops 13630592 | bytes 13635072 | tf_op jit(solution)/shard_map/reduce_sum | solution.py:78
  146.2 6.4 %fusion.49 = (f32[128]{0:T(128)S(1)}, f32[128]{0:T(128)S(1)}, f32[128]{0:T(128)S(1)}, f32[128]{0:T(128)S(1)}, f32[128]{0:T(128)S(1)}, /*index=5*/f32[128]{0:T(128)S(1)}) fusion(f32[128,4,6]{0,2,1:T(8,128)S(1)} %copy-done.79, f32[128,4,1018]{0,2,1:T(8,128)} %copy-done.12, bf16[4,128,4,1024]{1,3,2,0:T(8,128)(2,1)} %copy-done.2, ...), kind=kLoop, calls=%fused_computation.85 | loop fusion | flops 11009280 | bytes 13634560 | tf_op jit(solution)/shard_map/reduce_sum | solution.py:78
  152.8 3.2 reshape.53
  156.1 2.7 fusion.84
  158.9 1.9 collective-permute-start.17
  160.9 1.9 collective-permute-start.10
  162.8 2.2 collective-permute-start.11
  165.0 1.6 fusion.92
  166.9 2.2 fusion.88
  169.1 2.5 collective-permute-start.18
  171.7 3.4 collective-permute-start.16
  175.1 11.5 %collective-permute-done.10 = bf16[128,2,1024]{0,2,1:T(8,128)(2,1)S(1)} collective-permute-done((bf16[128,2,1024]{0,2,1:T(8,128)(2,1)S(1)}, bf16[128,2,1024]{0,2,1:T(8,128)(2,1)S(1)}, u32[]{:S(2)}, u32[]{:S(2)}) %collective-permute-start.10) | collective-permute-done | bytes 524320 | tf_op jit(solution)/shard_map/ppermute | solution.py:15
  186.6 1.9 collective-permute-start.19
  188.6 17.6 %collective-permute-done.11 = bf16[128,2,1024]{0,2,1:T(8,128)(2,1)S(1)} collective-permute-done((bf16[128,2,1024]{0,2,1:T(8,128)(2,1)S(1)}, bf16[128,2,1024]{0,2,1:T(8,128)(2,1)S(1)}, u32[]{:S(2)}, u32[]{:S(2)}) %collective-permute-start.11) | collective-permute-done | bytes 524320 | tf_op jit(solution)/shard_map/ppermute | solution.py:15
  206.2 1.9 collective-permute-start.12
  208.3 1.9 collective-permute-start.13
  210.2 1.9 collective-permute-start.15
  212.3 30.9 %collective-permute-start.14 = (bf16[128,4,1024]{0,2,1:T(8,128)(2,1)S(1)}, bf16[128,4,1024]{0,2,1:T(8,128)(2,1)S(1)}, u32[]{:S(2)}, u32[]{:S(2)}) collective-permute-start(bf16[128,4,1024]{0,2,1:T(8,128)(2,1)S(1)} %get-tuple-element.47), channel_id=1, source_target_pairs={{6,0},{8,2},{10,4},{12,6},{14,8},{16,10},{18,12},{20,14},{22,16},{... | collective-permute-start | bytes 3145736 | tf_op jit(solution)/shard_map/ppermute | solution.py:15
  243.4 2.3 fusion.90
  245.7 2.2 fusion.86
  247.9 11.1 %collective-permute-done.13 = bf16[128,2,1024]{0,2,1:T(8,128)(2,1)S(1)} collective-permute-done((bf16[128,2,1024]{0,2,1:T(8,128)(2,1)S(1)}, bf16[128,2,1024]{0,2,1:T(8,128)(2,1)S(1)}, u32[]{:S(2)}, u32[]{:S(2)}) %collective-permute-start.13) | collective-permute-done | bytes 524320 | tf_op jit(solution)/shard_map/ppermute | solution.py:15
  260.4 26.6 %collective-permute-done.15 = bf16[128,4,1024]{0,2,1:T(8,128)(2,1)S(1)} collective-permute-done((bf16[128,4,1024]{0,2,1:T(8,128)(2,1)S(1)}, bf16[128,4,1024]{0,2,1:T(8,128)(2,1)S(1)}, u32[]{:S(2)}, u32[]{:S(2)}) %collective-permute-start.15) | collective-permute-done | bytes 1048608 | tf_op jit(solution)/shard_map/ppermute | solution.py:15
  287.1 2.3 fusion.111
  289.4 2.4 fusion.109
  291.7 1.3 copy-done.3
  293.2 15.8 %fusion.40 = f32[128,4,1024]{0,2,1:T(8,128)} fusion(f32[128,4,6]{0,2,1:T(8,128)S(1)} %get-tuple-element.74, f32[128,4,1018]{0,2,1:T(8,128)S(1)} %get-tuple-element.76, f32[128,4,1018]{0,2,1:T(8,128)S(1)} %get-tuple-element.75, f32[128,4,6]{0,2,1:T(8,128)S(1)} %get-tuple-element.73, f32[128,4,6]{0,2,1:T(8,128)S(1)} %get-tuple-element.70, ...), kind=kLoop, calls=%fused_computation.76 | loop fusion | flops 45088768 | bytes 50345472 | tf_op jit(solution)/shard_map/add | solution.py:74
  309.0 3.0 copy.47
  312.1 1.6 copy.57
  313.7 1.7 copy.46
  315.4 41.2 %reduce_sum.279 = f32[134528]{0:T(1024)S(1)} reduce(f32[16,1,134528]{2,1,0:T(1,128)} %all-gather.7.cloned.1.call-done, f32[]{:T(128)} %constant.2.clone.1), dimensions={0,1}, to_apply=%region_28.29 | reduce | flops 2017920 | bytes 9147908 | tf_op jit(solution)/shard_map/reduce_sum | solution.py:86
  (309 shorter events, 15.7 us)
Async XLA Ops:
  7.2 109.4 %copy-start = (bf16[4,128,256]{2,1,0:T(8,128)(2,1)S(1)}, bf16[4,128,256]{2,1,0:T(8,128)(2,1)}, u32[]{:S(2)}) copy-start(bf16[4,128,256]{2,1,0:T(8,128)(2,1)} %param.6) | copy-start | bytes 786436
  7.2 14.8 %copy-start.55 = (bf16[128,4,1024]{2,1,0:T(4,128)(2,1)S(1)}, bf16[128,4,1024]{2,1,0:T(4,128)(2,1)}, u32[]{:S(2)}) copy-start(bf16[128,4,1024]{2,1,0:T(4,128)(2,1)} %param.7) | copy-start | bytes 3145732
  7.2 116.3 %all-gather.5.cloned.1.call-start = ((), (), s32[]{:S(2)}) async-start(), calls=%async_computation.1 | async-start | bytes 3145728 | tf_op jit(solution)/shard_map/all_gather | solution.py:58
  10.3 55.3 %collective-permute-start.8 = (bf16[128,2,1024]{0,2,1:T(8,128)(2,1)}, bf16[128,2,1024]{0,2,1:T(8,128)(2,1)}, u32[]{:S(2)}, u32[]{:S(2)}) collective-permute-start(bf16[128,2,1024]{0,2,1:T(8,128)(2,1)} %get-tuple-element.125), channel_id=1, source_target_pairs={{8,0},{10,2},{12,4},{14,6},{16,8},{18,10},{20,12},{22,14},{24,16},... | collective-permute-start | bytes 1572872 | tf_op jit(solution)/shard_map/ppermute | solution.py:15
  12.7 17.8 %collective-permute-start.6 = (bf16[128,2,1024]{0,2,1:T(8,128)(2,1)}, bf16[128,2,1024]{0,2,1:T(8,128)(2,1)S(1)}, u32[]{:S(2)}, u32[]{:S(2)}) collective-permute-start(bf16[128,2,1024]{0,2,1:T(8,128)(2,1)} %get-tuple-element.125), channel_id=1, source_target_pairs={{0,10},{2,12},{4,14},{6,16},{8,18},{10,20},{12,22},{14,24},{16,26}... | collective-permute-start | bytes 1572872 | tf_op jit(solution)/shard_map/ppermute | solution.py:15
  16.1 59.1 %collective-permute-start.2 = (bf16[128,2,1024]{0,2,1:T(8,128)(2,1)}, bf16[128,2,1024]{0,2,1:T(8,128)(2,1)}, u32[]{:S(2)}, u32[]{:S(2)}) collective-permute-start(bf16[128,2,1024]{0,2,1:T(8,128)(2,1)} %get-tuple-element.125), channel_id=1, source_target_pairs={{2,0},{4,2},{6,4},{8,6},{10,8},{12,10},{14,12},{16,14},{18,16},{20... | collective-permute-start | bytes 1572872 | tf_op jit(solution)/shard_map/ppermute | solution.py:15
  20.1 61.3 %collective-permute-start = (bf16[128,2,1024]{0,2,1:T(8,128)(2,1)}, bf16[128,2,1024]{0,2,1:T(8,128)(2,1)}, u32[]{:S(2)}, u32[]{:S(2)}) collective-permute-start(bf16[128,2,1024]{0,2,1:T(8,128)(2,1)} %get-tuple-element.125), channel_id=1, source_target_pairs={{0,4},{2,6},{4,8},{6,10},{8,12},{10,14},{12,16},{14,18},{16,20},{1... | collective-permute-start | bytes 1572872 | tf_op jit(solution)/shard_map/ppermute | solution.py:15
  23.4 288.6 %reduce-scatter.4.cloned.1.call-start = ((), (), s32[]{:S(2)}) async-start(), calls=%async_computation.3 | async-start | bytes 3145728
  23.5 36.7 %collective-permute-start.7 = (bf16[128,2,1024]{0,2,1:T(8,128)(2,1)}, bf16[128,2,1024]{0,2,1:T(8,128)(2,1)S(1)}, u32[]{:S(2)}, u32[]{:S(2)}) collective-permute-start(bf16[128,2,1024]{0,2,1:T(8,128)(2,1)} %get-tuple-element.126), channel_id=1, source_target_pairs={{0,8},{2,10},{4,12},{6,14},{8,16},{10,18},{12,20},{14,22},{16,24},... | collective-permute-start | bytes 1572872 | tf_op jit(solution)/shard_map/ppermute | solution.py:15
  25.4 81.2 %copy-start.74 = (f32[128,4,6]{0,2,1:T(8,128)}, f32[128,4,6]{0,2,1:T(8,128)S(1)}, u32[]{:S(2)}) copy-start(f32[128,4,6]{0,2,1:T(8,128)S(1)} %get-tuple-element.105) | copy-start | bytes 36868
  25.4 81.2 %copy-start.76 = (f32[128,4,6]{0,2,1:T(8,128)}, f32[128,4,6]{0,2,1:T(8,128)S(1)}, u32[]{:S(2)}) copy-start(f32[128,4,6]{0,2,1:T(8,128)S(1)} %get-tuple-element.106) | copy-start | bytes 36868
  25.4 87.2 %copy-start.62 = (f32[128,4,12]{0,2,1:T(8,128)}, f32[128,4,12]{0,2,1:T(8,128)S(1)}, u32[]{:S(2)}) copy-start(f32[128,4,12]{0,2,1:T(8,128)S(1)} %get-tuple-element.113) | copy-start | bytes 73732
  25.4 87.2 %copy-start.64 = (f32[128,4,12]{0,2,1:T(8,128)}, f32[128,4,12]{0,2,1:T(8,128)S(1)}, u32[]{:S(2)}) copy-start(f32[128,4,12]{0,2,1:T(8,128)S(1)} %get-tuple-element.114) | copy-start | bytes 73732
  25.8 72.8 %copy-start.27 = (f32[128,4,1006]{0,2,1:T(8,128)}, f32[128,4,1006]{0,2,1:T(8,128)S(1)}, u32[]{:S(2)}) copy-start(f32[128,4,1006]{0,2,1:T(8,128)S(1)} %get-tuple-element.123) | copy-start | bytes 6180868
  25.8 72.8 %copy-start.28 = (f32[128,4,1006]{0,2,1:T(8,128)}, f32[128,4,1006]{0,2,1:T(8,128)S(1)}, u32[]{:S(2)}) copy-start(f32[128,4,1006]{0,2,1:T(8,128)S(1)} %get-tuple-element.124) | copy-start | bytes 6180868
  26.5 86.1 %copy-start.15 = (f32[128,4,1012]{0,2,1:T(8,128)}, f32[128,4,1012]{0,2,1:T(8,128)S(1)}, u32[]{:S(2)}) copy-start(f32[128,4,1012]{0,2,1:T(8,128)S(1)} %get-tuple-element.115) | copy-start | bytes 6217732
  26.5 86.1 %copy-start.17 = (f32[128,4,1012]{0,2,1:T(8,128)}, f32[128,4,1012]{0,2,1:T(8,128)S(1)}, u32[]{:S(2)}) copy-start(f32[128,4,1012]{0,2,1:T(8,128)S(1)} %get-tuple-element.116) | copy-start | bytes 6217732
  27.6 71.0 %copy-start.89 = (f32[128]{0:T(128)}, f32[128]{0:T(128)S(1)}, u32[]{:S(2)}) copy-start(f32[128]{0:T(128)S(1)} %get-tuple-element.128) | copy-start | bytes 1540
  27.6 71.0 %copy-start.90 = (f32[128]{0:T(128)}, f32[128]{0:T(128)S(1)}, u32[]{:S(2)}) copy-start(f32[128]{0:T(128)S(1)} %get-tuple-element.129) | copy-start | bytes 1540
  27.6 71.0 %copy-start.91 = (f32[128]{0:T(128)}, f32[128]{0:T(128)S(1)}, u32[]{:S(2)}) copy-start(f32[128]{0:T(128)S(1)} %get-tuple-element.130) | copy-start | bytes 1540
  27.6 71.0 %copy-start.92 = (f32[128]{0:T(128)}, f32[128]{0:T(128)S(1)}, u32[]{:S(2)}) copy-start(f32[128]{0:T(128)S(1)} %get-tuple-element.131) | copy-start | bytes 1540
  27.6 71.0 %copy-start.93 = (f32[128]{0:T(128)}, f32[128]{0:T(128)S(1)}, u32[]{:S(2)}) copy-start(f32[128]{0:T(128)S(1)} %get-tuple-element.132) | copy-start | bytes 1540
  27.7 71.0 %copy-start.94 = (f32[128]{0:T(128)}, f32[128]{0:T(128)S(1)}, u32[]{:S(2)}) copy-start(f32[128]{0:T(128)S(1)} %get-tuple-element.133) | copy-start | bytes 1540
  27.7 71.0 %copy-start.95 = (f32[128]{0:T(128)}, f32[128]{0:T(128)S(1)}, u32[]{:S(2)}) copy-start(f32[128]{0:T(128)S(1)} %get-tuple-element.134) | copy-start | bytes 1540
  27.7 71.0 %copy-start.96 = (f32[128]{0:T(128)}, f32[128]{0:T(128)S(1)}, u32[]{:S(2)}) copy-start(f32[128]{0:T(128)S(1)} %get-tuple-element.135) | copy-start | bytes 1540
  27.7 71.0 %copy-start.97 = (f32[128]{0:T(128)}, f32[128]{0:T(128)S(1)}, u32[]{:S(2)}) copy-start(f32[128]{0:T(128)S(1)} %get-tuple-element.136) | copy-start | bytes 1540
  27.7 79.0 %copy-start.87 = (f32[128]{0:T(128)}, f32[128]{0:T(128)S(1)}, u32[]{:S(2)}) copy-start(f32[128]{0:T(128)S(1)} %get-tuple-element.127) | copy-start | bytes 1540
  29.0 77.7 %copy-start.4 = (f32[128,4,1018]{0,2,1:T(8,128)}, f32[128,4,1018]{0,2,1:T(8,128)S(1)}, u32[]{:S(2)}) copy-start(f32[128,4,1018]{0,2,1:T(8,128)S(1)} %get-tuple-element.107) | copy-start | bytes 6254596
  29.0 77.7 %copy-start.6 = (f32[128,4,1018]{0,2,1:T(8,128)}, f32[128,4,1018]{0,2,1:T(8,128)S(1)}, u32[]{:S(2)}) copy-start(f32[128,4,1018]{0,2,1:T(8,128)S(1)} %get-tuple-element.108) | copy-start | bytes 6254596
  30.4 29.7 %copy-start.31 = (bf16[128,2,1024]{0,2,1:T(8,128)(2,1)}, bf16[128,2,1024]{0,2,1:T(8,128)(2,1)S(1)}, u32[]{:S(2)}) copy-start(bf16[128,2,1024]{0,2,1:T(8,128)(2,1)S(1)} %collective-permute-done.6) | copy-start | bytes 1572868
  30.4 38.5 %collective-permute-start.9 = (bf16[128,2,1024]{0,2,1:T(8,128)(2,1)}, bf16[128,2,1024]{0,2,1:T(8,128)(2,1)S(1)}, u32[]{:S(2)}, u32[]{:S(2)}) collective-permute-start(bf16[128,2,1024]{0,2,1:T(8,128)(2,1)} %get-tuple-element.126), channel_id=1, source_target_pairs={{10,0},{12,2},{14,4},{16,6},{18,8},{20,10},{22,12},{24,14},{26,16}... | collective-permute-start | bytes 1572872 | tf_op jit(solution)/shard_map/ppermute | solution.py:15
  60.1 38.6 %copy-start.34 = (bf16[128,2,1024]{0,2,1:T(8,128)(2,1)}, bf16[128,2,1024]{0,2,1:T(8,128)(2,1)S(1)}, u32[]{:S(2)}) copy-start(bf16[128,2,1024]{0,2,1:T(8,128)(2,1)S(1)} %collective-permute-done.7) | copy-start | bytes 1572868
  60.1 19.5 %collective-permute-start.3 = (bf16[128,2,1024]{0,2,1:T(8,128)(2,1)}, bf16[128,2,1024]{0,2,1:T(8,128)(2,1)S(1)}, u32[]{:S(2)}, u32[]{:S(2)}) collective-permute-start(bf16[128,2,1024]{0,2,1:T(8,128)(2,1)} %get-tuple-element.126), channel_id=1, source_target_pairs={{4,0},{6,2},{8,4},{10,6},{12,8},{14,10},{16,12},{18,14},{20,16},{2... | collective-permute-start | bytes 1572872 | tf_op jit(solution)/shard_map/ppermute | solution.py:15
  63.2 35.5 %copy-start.58 = (f32[128,4,18]{0,2,1:T(8,128)}, f32[128,4,18]{0,2,1:T(8,128)S(1)}, u32[]{:S(2)}) copy-start(f32[128,4,18]{0,2,1:T(8,128)S(1)} %get-tuple-element.85) | copy-start | bytes 110596
  63.2 35.5 %copy-start.60 = (f32[128,4,18]{0,2,1:T(8,128)}, f32[128,4,18]{0,2,1:T(8,128)S(1)}, u32[]{:S(2)}) copy-start(f32[128,4,18]{0,2,1:T(8,128)S(1)} %get-tuple-element.86) | copy-start | bytes 110596
  65.6 30.7 %collective-permute-start.1 = (bf16[128,2,1024]{0,2,1:T(8,128)(2,1)}, bf16[128,2,1024]{0,2,1:T(8,128)(2,1)S(1)}, u32[]{:S(2)}, u32[]{:S(2)}) collective-permute-start(bf16[128,2,1024]{0,2,1:T(8,128)(2,1)} %get-tuple-element.126), channel_id=1, source_target_pairs={{0,2},{2,4},{4,6},{6,8},{8,10},{10,12},{12,14},{14,16},{16,18},{18... | collective-permute-start | bytes 1572872 | tf_op jit(solution)/shard_map/ppermute | solution.py:15
  68.9 29.8 %copy-start.36 = (bf16[128,2,1024]{0,2,1:T(8,128)(2,1)}, bf16[128,2,1024]{0,2,1:T(8,128)(2,1)S(1)}, u32[]{:S(2)}) copy-start(bf16[128,2,1024]{0,2,1:T(8,128)(2,1)S(1)} %collective-permute-done.9) | copy-start | bytes 1572868
  68.9 42.9 %collective-permute-start.5 = (bf16[128,4,1024]{0,2,1:T(8,128)(2,1)S(1)}, bf16[128,4,1024]{0,2,1:T(8,128)(2,1)S(1)}, u32[]{:S(2)}, u32[]{:S(2)}) collective-permute-start(bf16[128,4,1024]{0,2,1:T(8,128)(2,1)S(1)} %copy.35), channel_id=1, source_target_pairs={{6,0},{8,2},{10,4},{12,6},{14,8},{16,10},{18,12},{20,14},{22,16},{... | collective-permute-start | bytes 3145736 | tf_op jit(solution)/shard_map/ppermute | solution.py:15
  72.9 25.8 %copy-start.56 = (f32[128,4,18]{0,2,1:T(8,128)}, f32[128,4,18]{0,2,1:T(8,128)S(1)}, u32[]{:S(2)}) copy-start(f32[128,4,18]{0,2,1:T(8,128)S(1)} %get-tuple-element.90) | copy-start | bytes 110596
  75.2 36.7 %collective-permute-start.4 = (bf16[128,4,1024]{0,2,1:T(8,128)(2,1)S(1)}, bf16[128,4,1024]{0,2,1:T(8,128)(2,1)S(1)}, u32[]{:S(2)}, u32[]{:S(2)}) collective-permute-start(bf16[128,4,1024]{0,2,1:T(8,128)(2,1)S(1)} %copy.35), channel_id=1, source_target_pairs={{0,6},{2,8},{4,10},{6,12},{8,14},{10,16},{12,18},{14,20},{16,22},{... | collective-permute-start | bytes 3145736 | tf_op jit(solution)/shard_map/ppermute | solution.py:15
  81.3 25.4 %copy-start.12 = (f32[128,4,1018]{0,2,1:T(8,128)}, f32[128,4,1018]{0,2,1:T(8,128)S(1)}, u32[]{:S(2)}) copy-start(f32[128,4,1018]{0,2,1:T(8,128)S(1)} %get-tuple-element.84) | copy-start | bytes 6254596
  81.3 25.4 %copy-start.13 = (f32[128,4,1018]{0,2,1:T(8,128)}, f32[128,4,1018]{0,2,1:T(8,128)S(1)}, u32[]{:S(2)}) copy-start(f32[128,4,1018]{0,2,1:T(8,128)S(1)} %get-tuple-element.83) | copy-start | bytes 6254596
  98.6 8.2 %copy-start.8 = (f32[128,4,1018]{0,2,1:T(8,128)}, f32[128,4,1018]{0,2,1:T(8,128)S(1)}, u32[]{:S(2)}) copy-start(f32[128,4,1018]{0,2,1:T(8,128)S(1)} %get-tuple-element.79) | copy-start | bytes 6254596
  98.6 8.2 %copy-start.10 = (f32[128,4,1018]{0,2,1:T(8,128)}, f32[128,4,1018]{0,2,1:T(8,128)S(1)}, u32[]{:S(2)}) copy-start(f32[128,4,1018]{0,2,1:T(8,128)S(1)} %get-tuple-element.80) | copy-start | bytes 6254596
  123.2 192.2 %all-gather.7.cloned.1.call-start = ((), (), s32[]{:S(2)}) async-start(), calls=%async_computation.2 | async-start | bytes 9147904 | tf_op jit(solution)/shard_map/all_gather | solution.py:86
  123.5 6.5 %copy-start.22 = (f32[128,4,1012]{0,2,1:T(8,128)S(1)}, f32[128,4,1012]{0,2,1:T(8,128)}, u32[]{:S(2)}) copy-start(f32[128,4,1012]{0,2,1:T(8,128)} %copy-done.21) | copy-start | bytes 6217732
  132.2 9.9 %copy-start.2 = (bf16[4,128,4,1024]{1,3,2,0:T(8,128)(2,1)}, bf16[4,128,4,1024]{1,3,2,0:T(8,128)(2,1)S(1)}, u32[]{:S(2)}) copy-start(bf16[4,128,4,1024]{1,3,2,0:T(8,128)(2,1)S(1)} %convolution_convert_fusion) | copy-start | bytes 12582916
  146.2 6.5 %copy-start.108 = (f32[128]{0:T(128)S(1)}, f32[128]{0:T(128)}, u32[]{:S(2)}) copy-start(f32[128]{0:T(128)} %get-tuple-element.18) | copy-start | bytes 1540
  146.2 6.5 %copy-start.51 = (f32[64,2,8,128]{3,1,2,0:T(2,128)S(1)}, f32[64,2,8,128]{3,1,2,0:T(2,128)}, u32[]{:S(2)}) copy-start(f32[64,2,8,128]{3,1,2,0:T(2,128)} %copy.58) | copy-start | bytes 1572868
  158.9 51.3 %collective-permute-start.17 = (bf16[128,2,1024]{0,2,1:T(8,128)(2,1)S(1)}, bf16[128,2,1024]{0,2,1:T(8,128)(2,1)S(1)}, u32[]{:S(2)}, u32[]{:S(2)}) collective-permute-start(bf16[128,2,1024]{0,2,1:T(8,128)(2,1)S(1)} %get-tuple-element.94), channel_id=1, source_target_pairs={{10,0},{12,2},{14,4},{16,6},{18,8},{20,10},{22,12},{24,14},{26,16}... | collective-permute-start | bytes 1572872 | tf_op jit(solution)/shard_map/ppermute | solution.py:15
  160.9 25.7 %collective-permute-start.10 = (bf16[128,2,1024]{0,2,1:T(8,128)(2,1)S(1)}, bf16[128,2,1024]{0,2,1:T(8,128)(2,1)S(1)}, u32[]{:S(2)}, u32[]{:S(2)}) collective-permute-start(bf16[128,2,1024]{0,2,1:T(8,128)(2,1)S(1)} %get-tuple-element.103), channel_id=1, source_target_pairs={{2,0},{4,2},{6,4},{8,6},{10,8},{12,10},{14,12},{16,14},{18,16},{20... | collective-permute-start | bytes 1572872 | tf_op jit(solution)/shard_map/ppermute | solution.py:15
  162.8 43.4 %collective-permute-start.11 = (bf16[128,2,1024]{0,2,1:T(8,128)(2,1)S(1)}, bf16[128,2,1024]{0,2,1:T(8,128)(2,1)S(1)}, u32[]{:S(2)}, u32[]{:S(2)}) collective-permute-start(bf16[128,2,1024]{0,2,1:T(8,128)(2,1)S(1)} %get-tuple-element.104), channel_id=1, source_target_pairs={{4,0},{6,2},{8,4},{10,6},{12,8},{14,10},{16,12},{18,14},{20,16},{2... | collective-permute-start | bytes 1572872 | tf_op jit(solution)/shard_map/ppermute | solution.py:15
  169.1 43.2 %collective-permute-start.18 = (bf16[128,2,1024]{0,2,1:T(8,128)(2,1)S(1)}, bf16[128,2,1024]{0,2,1:T(8,128)(2,1)S(1)}, u32[]{:S(2)}, u32[]{:S(2)}) collective-permute-start(bf16[128,2,1024]{0,2,1:T(8,128)(2,1)S(1)} %get-tuple-element.93), channel_id=1, source_target_pairs={{0,10},{2,12},{4,14},{6,16},{8,18},{10,20},{12,22},{14,24},{16,26}... | collective-permute-start | bytes 1572872 | tf_op jit(solution)/shard_map/ppermute | solution.py:15
  171.7 36.6 %collective-permute-start.16 = (bf16[128,2,1024]{0,2,1:T(8,128)(2,1)S(1)}, bf16[128,2,1024]{0,2,1:T(8,128)(2,1)S(1)}, u32[]{:S(2)}, u32[]{:S(2)}) collective-permute-start(bf16[128,2,1024]{0,2,1:T(8,128)(2,1)S(1)} %get-tuple-element.93), channel_id=1, source_target_pairs={{8,0},{10,2},{12,4},{14,6},{16,8},{18,10},{20,12},{22,14},{24,16},... | collective-permute-start | bytes 1572872 | tf_op jit(solution)/shard_map/ppermute | solution.py:15
  186.6 56.6 %collective-permute-start.19 = (bf16[128,2,1024]{0,2,1:T(8,128)(2,1)S(1)}, bf16[128,2,1024]{0,2,1:T(8,128)(2,1)S(1)}, u32[]{:S(2)}, u32[]{:S(2)}) collective-permute-start(bf16[128,2,1024]{0,2,1:T(8,128)(2,1)S(1)} %get-tuple-element.94), channel_id=1, source_target_pairs={{0,8},{2,10},{4,12},{6,14},{8,16},{10,18},{12,20},{14,22},{16,24},... | collective-permute-start | bytes 1572872 | tf_op jit(solution)/shard_map/ppermute | solution.py:15
  206.2 41.7 %collective-permute-start.12 = (bf16[128,2,1024]{0,2,1:T(8,128)(2,1)S(1)}, bf16[128,2,1024]{0,2,1:T(8,128)(2,1)S(1)}, u32[]{:S(2)}, u32[]{:S(2)}) collective-permute-start(bf16[128,2,1024]{0,2,1:T(8,128)(2,1)S(1)} %get-tuple-element.103), channel_id=1, source_target_pairs={{0,4},{2,6},{4,8},{6,10},{8,12},{10,14},{12,16},{14,18},{16,20},{1... | collective-permute-start | bytes 1572872 | tf_op jit(solution)/shard_map/ppermute | solution.py:15
  208.3 35.1 %copy-start.46 = (bf16[128,2,1024]{0,2,1:T(8,128)(2,1)}, bf16[128,2,1024]{0,2,1:T(8,128)(2,1)S(1)}, u32[]{:S(2)}) copy-start(bf16[128,2,1024]{0,2,1:T(8,128)(2,1)S(1)} %collective-permute-done.16) | copy-start | bytes 1572868
  208.3 50.7 %collective-permute-start.13 = (bf16[128,2,1024]{0,2,1:T(8,128)(2,1)S(1)}, bf16[128,2,1024]{0,2,1:T(8,128)(2,1)S(1)}, u32[]{:S(2)}, u32[]{:S(2)}) collective-permute-start(bf16[128,2,1024]{0,2,1:T(8,128)(2,1)S(1)} %get-tuple-element.104), channel_id=1, source_target_pairs={{0,2},{2,4},{4,6},{6,8},{8,10},{10,12},{12,14},{14,16},{16,18},{18... | collective-permute-start | bytes 1572872 | tf_op jit(solution)/shard_map/ppermute | solution.py:15
  210.2 33.0 %copy-start.42 = (bf16[128,2,1024]{0,2,1:T(8,128)(2,1)}, bf16[128,2,1024]{0,2,1:T(8,128)(2,1)S(1)}, u32[]{:S(2)}) copy-start(bf16[128,2,1024]{0,2,1:T(8,128)(2,1)S(1)} %collective-permute-done.17) | copy-start | bytes 1572868
  210.2 76.8 %collective-permute-start.15 = (bf16[128,4,1024]{0,2,1:T(8,128)(2,1)S(1)}, bf16[128,4,1024]{0,2,1:T(8,128)(2,1)S(1)}, u32[]{:S(2)}, u32[]{:S(2)}) collective-permute-start(bf16[128,4,1024]{0,2,1:T(8,128)(2,1)S(1)} %get-tuple-element.47), channel_id=1, source_target_pairs={{0,6},{2,8},{4,10},{6,12},{8,14},{10,16},{12,18},{14,20},{16,22},{... | collective-permute-start | bytes 3145736 | tf_op jit(solution)/shard_map/ppermute | solution.py:15
  212.3 33.4 %copy-start.45 = (bf16[128,2,1024]{0,2,1:T(8,128)(2,1)}, bf16[128,2,1024]{0,2,1:T(8,128)(2,1)S(1)}, u32[]{:S(2)}) copy-start(bf16[128,2,1024]{0,2,1:T(8,128)(2,1)S(1)} %collective-permute-done.18) | copy-start | bytes 1572868
  212.3 74.7 %collective-permute-start.14 = (bf16[128,4,1024]{0,2,1:T(8,128)(2,1)S(1)}, bf16[128,4,1024]{0,2,1:T(8,128)(2,1)S(1)}, u32[]{:S(2)}, u32[]{:S(2)}) collective-permute-start(bf16[128,4,1024]{0,2,1:T(8,128)(2,1)S(1)} %get-tuple-element.47), channel_id=1, source_target_pairs={{6,0},{8,2},{10,4},{12,6},{14,8},{16,10},{18,12},{20,14},{22,16},{... | collective-permute-start | bytes 3145736 | tf_op jit(solution)/shard_map/ppermute | solution.py:15
  247.9 11.2 %copy-start.48 = (bf16[128,2,1024]{0,2,1:T(8,128)(2,1)}, bf16[128,2,1024]{0,2,1:T(8,128)(2,1)S(1)}, u32[]{:S(2)}) copy-start(bf16[128,2,1024]{0,2,1:T(8,128)(2,1)S(1)} %collective-permute-done.12) | copy-start | bytes 1572868
  315.4 42.8 %copy-start.1 = (bf16[4,128,256]{2,1,0:T(8,128)(2,1)S(1)}, bf16[4,128,256]{2,1,0:T(8,128)(2,1)}, u32[]{:S(2)}) copy-start(bf16[4,128,256]{2,1,0:T(8,128)(2,1)} %param.6) | copy-start | bytes 786436
  (80 other events, 300.7 us)
Sparse Core Ops, SparseCore 0:
  23.5 34.5 all-gather.4
  123.3 31.9 reduce-scatter.3
  157.6 120.4 all-gather.6
